TPU v7x, 32 devices: a whole 2x2x4 slice. The times are simulated.
32 devices in a mesh: parts: 2 (over y), filt: 4 (over z), space: 4 (over x, core).
Axes of the slice: x: 2, y: 2, z: 4, core: 2. Of those that a mesh axis runs over, the one named last changes fastest.
Arguments:
- volume: bfloat16 [512, 16, 8, 128], P('filt', ('parts', 'space')), parts along dimension 1, may hold values from -6 to 6
- weight: bfloat16 [512, 27, 512], P('filt'), may hold values from -0.0546875 to 0.0546875
- bias: float32 [512], P('filt'), may hold values from -3 to 3
- upstream: bfloat16 [512, 16, 8, 128], P('filt', ('parts', 'space')), parts along dimension 1, may hold values from -0.0625 to 0.0625
Outputs:
- features: bfloat16 [512, 16, 8, 128], P('filt', ('parts', 'space')), parts along dimension 1
- weight_grad: float32 [1024, 27, 512], P(('parts', 'filt')), parts along dimension 0
There are 2 independent parts, one for each index of `parts`. A program takes and returns all parts, laid end to end along the dimension named above; an argument that names none is the same for every part. Nothing has to cross between parts.
All inputs are finite; a program needn't handle non-finite values.
Results may differ from a plain program's by a relative error of at most 0.001.
Values may be sent and summed in bfloat16 or wider, within the bound.
No kernel may reach another device: no remote copies, remote signals or barrier semaphores. Data moves between devices by JAX's collectives and lax.ppermute only.
A program may use at most 128 MiB of HBM per device.

v0:
```python
import jax
import jax.numpy as jnp
from jax import lax
from jax.sharding import PartitionSpec as P


def padded(block, sides, width):
    for axis, dim in sides:
        count = lax.axis_size(axis)
        forward = [(i, i + 1) for i in range(count - 1)]
        backward = [(target, source) for source, target in forward]
        low = lax.ppermute(
            lax.slice_in_dim(block, block.shape[dim] - width, None, axis=dim), axis, forward
        )
        high = lax.ppermute(lax.slice_in_dim(block, 0, width, axis=dim), axis, backward)
        block = jnp.concatenate([low, block, high], axis=dim)
    return block


def convolve(slab, kernel):
    return lax.conv_general_dilated(
        slab[None],
        kernel,
        (1, 1, 1),
        [(0, 0), (1, 1), (1, 1)],
        dimension_numbers=("NCDHW", "OIDHW", "NCDHW"),
        preferred_element_type=jnp.float32,
    )[0]


def shifted_slopes(upstream):
    out_dev = upstream.shape[0]
    depth = upstream.shape[1]
    height = upstream.shape[2]
    length = upstream.shape[3]
    spread = jnp.pad(upstream, ((0, 0), (2, 2), (1, 1), (1, 1)))
    copies = []
    for tap in range(27):
        first = tap // 9
        second = tap // 3 % 3
        third = tap % 3
        copies.append(
            spread[
                :,
                2 - first : 4 - first + depth,
                2 - second : 2 - second + height,
                2 - third : 2 - third + length,
            ]
        )
    stacked = jnp.stack(copies, 1)
    return stacked.reshape(out_dev * 27, (depth + 2) * height * length)


def tap_grads(slab, slopes, out_dev):
    flat = slab.reshape(slab.shape[0], -1)
    product = lax.dot_general(
        slopes, flat, (((1,), (1,)), ((), ())), preferred_element_type=jnp.float32
    )
    return product.reshape(out_dev, 27, slab.shape[0])


def on_device(volume, weight, bias, upstream):
    out_dev = weight.shape[0]
    in_all = weight.shape[2]
    kernel = weight.reshape(out_dev, 3, 3, 3, in_all).transpose(0, 4, 1, 2, 3)
    slopes = shifted_slopes(upstream)
    whole = lax.all_gather(volume, "filt", axis=0, tiled=True)
    rimmed = padded(whole, (("space", 1),), 1)
    pre = convolve(rimmed, kernel)
    partial_grads = tap_grads(rimmed, slopes, out_dev)
    weight_grad = lax.psum(partial_grads, "space")
    pre = pre + bias[:, None, None, None]
    features = jnp.where(pre > 0, pre, 0.3 * pre).astype(jnp.bfloat16)
    return (features, weight_grad)


def solution(mesh):
    return jax.shard_map(
        on_device,
        mesh=mesh,
        in_specs=(
            P("filt", ("parts", "space"), None, None),
            P("filt", None, None),
            P("filt"),
            P("filt", ("parts", "space"), None, None),
        ),
        out_specs=(P("filt", ("parts", "space"), None, None), P(("parts", "filt"), None, None)),
        check_vma=False,
    )
```

profile of v0, /device:TPU:0, one launch (start us, length us, event | category | flops | bytes accessed | tf_op | source)
XLA Modules:
  0.0 254.6 jit_solution(8644923369791404062)
XLA Ops:
  7.2 2.1 copy.8
  13.1 1.3 fusion.23
  14.3 1.3 fusion.25
  16.8 1.3 fusion.29
  18.1 1.3 fusion.31
  20.5 1.4 fusion.35
  24.3 1.3 fusion.41
  25.6 1.4 fusion.43
  31.8 1.3 fusion.53
  33.1 1.3 fusion.55
  34.4 24.5 %all-gather.2.cloned.1.call-done = bf16[512,2,8,128]{3,0,2,1:T(8,128)(2,1)} async-done(((bf16[128,2,8,128]{3,0,2,1:T(8,128)(2,1)}), bf16[512,2,8,128]{3,0,2,1:T(8,128)(2,1)}) %all-gather.2.cloned.1.call-update) | async-done | bytes 2097168 | tf_op jit(solution)/shard_map/all_gather | solution.py:67
  58.8 1.7 fusion.76
  60.5 1.8 collective-permute-start
  62.3 2.2 fusion.57
  64.5 2.3 fusion.59
  66.8 1.3 collective-permute-start.1
  68.1 2.3 fusion.61
  70.4 2.2 fusion.63
  72.6 2.3 fusion.65
  75.0 2.4 fusion.67
  77.3 2.1 fusion.69
  79.5 2.3 fusion.71
  81.9 1.9 constant_dynamic-update-slice_fusion.1
  84.0 2.0 copy-done.2
  86.0 20.7 %fusion.10 = f32[128,27,512]{2,0,1:T(8,128)} fusion(bf16[128,27,4,8,128]{4,0,3,2,1:T(8,128)(2,1)} %fusion.71, bf16[512,4,8,128]{3,0,2,1:T(8,128)(2,1)S(1)} %constant_dynamic-update-slice_fusion), kind=kOutput, calls=%fused_computation.38 | convolution fusion | flops 14495514624 | bytes 39583744 | tf_op jit(solution)/shard_map/dot_general | solution.py:56
  106.7 8.0 %copy.18 = bf16[512,4,8,1,128]{0,2,4,1,3:T(8,128)(2,1)} copy(bf16[512,4,8,1,128]{4,0,2,1,3:T(8,128)(2,1)} %bitcast.144) | data formatting | bytes 8388608
  114.7 2.6 %pad.5.clone = bf16[512,4,8,1,136]{0,2,4,1,3:T(8,128)(2,1)S(1)} pad(bf16[512,4,8,1,128]{0,2,4,1,3:T(8,128)(2,1)} %copy.18, bf16[]{:T(256)} %constant.6.clone.1), padding=0_0x0_0x0_0x0_0x1_7 | pad | bytes 8650754 | tf_op jit(solution)/shard_map/broadcast_in_dim | solution.py:22
  117.3 1.7 copy.11
  119.2 16.9 %fusion.14 = f32[2,8,8,17,128]{4,2,3,1,0:T(8,128)S(1)} fusion(bf16[128,3,3,3,512]{4,0,3,2,1:T(8,128)(2,1)S(1)} %bitcast.142, bf16[512,4,8,1,7,2]{0,4,5,2,1,3:T(8,128)(2,1)S(1)} %slice.120, bf16[512,4,8,1,8,17]{0,4,5,2,1,3:T(8,128)(2,1)S(1)} %copy.11, pred[8,17]{0,1:T(8,128)(4,1)S(1)} %copy-done.4), kind=kOutput, calls=%fused_computation.40 | convolution fusion | flops 7074234368 | bytes 9568392 | tf_op jit(solution)/shard_map/conv_general_dilated | solution.py:21
  137.3 2.4 copy.14
  139.7 100.7 %all-reduce.3.cloned.1.call-done = f32[128,27,512]{2,0,1:T(8,128)} async-done(((f32[128,27,512]{2,0,1:T(8,128)}), f32[128,27,512]{2,0,1:T(8,128)}) %all-reduce.3.cloned.1.call-update) | async-done | bytes 7077904 | tf_op jit(solution)/shard_map/psum | solution.py:71
  240.4 7.3 %copy.48 = f32[128,27,512]{2,0,1:T(8,128)} copy(f32[128,27,512]{2,0,1:T(8,128)} %all-reduce.3.cloned.1.call-done) | data formatting | bytes 14155776
  (31 shorter events, 14.8 us)
Async XLA Ops:
  7.2 112.0 %copy-start = (bf16[128,27,512]{2,0,1:T(8,128)(2,1)S(1)}, bf16[128,27,512]{2,0,1:T(8,128)(2,1)}, u32[]{:S(2)}) copy-start(bf16[128,27,512]{2,0,1:T(8,128)(2,1)} %param.5) | copy-start | bytes 10616836
  7.2 51.7 %all-gather.2.cloned.1.call-start = ((), (), s32[]{:S(2)}) async-start(), calls=%async_computation | async-start | bytes 2621440 | tf_op jit(solution)/shard_map/all_gather | solution.py:67
  9.4 231.0 %all-reduce.3.cloned.1.call-start = ((), (), s32[]{:S(2)}) async-start(), calls=%async_computation.1 | async-start | bytes 14155776 | tf_op jit(solution)/shard_map/psum | solution.py:71
  10.6 22.5 %copy-start.1 = (bf16[128,2,8,128]{3,0,2,1:T(8,128)(2,1)}, bf16[128,2,8,128]{3,0,2,1:T(8,128)(2,1)S(1)}, u32[]{:S(2)}) copy-start(bf16[128,2,8,128]{3,0,2,1:T(8,128)(2,1)S(1)} %copy.13) | copy-start | bytes 1572868
  60.5 21.2 %collective-permute-start = (bf16[512,1,8,128]{3,0,2,1:T(8,128)(2,1)S(1)}, bf16[512,1,8,128]{3,0,2,1:T(8,128)(2,1)S(1)}, u32[]{:S(2)}, u32[]{:S(2)}) collective-permute-start(bf16[512,1,8,128]{3,0,2,1:T(8,128)(2,1)S(1)} %get-tuple-element.5), channel_id=1, source_target_pairs={{0,1},{1,2},{2,3},{4,5},{5,6},{6,7},{8,9},{9,10},{10,11},{12,13},{... | collective-permute-start | bytes 3145736 | tf_op jit(solution)/shard_map/ppermute | solution.py:12
  66.8 17.0 %collective-permute-start.1 = (bf16[512,1,8,128]{3,0,2,1:T(8,128)(2,1)S(1)}, bf16[512,1,8,128]{3,0,2,1:T(8,128)(2,1)S(1)}, u32[]{:S(2)}, u32[]{:S(2)}) collective-permute-start(bf16[512,1,8,128]{3,0,2,1:T(8,128)(2,1)S(1)} %get-tuple-element.4), channel_id=1, source_target_pairs={{1,0},{2,1},{3,2},{5,4},{6,5},{7,6},{9,8},{10,9},{11,10},{13,12},{... | collective-permute-start | bytes 3145736 | tf_op jit(solution)/shard_map/ppermute | solution.py:15
  83.9 2.0 copy-start.2
  106.6 12.6 %copy-start.4 = (pred[8,17]{0,1:T(8,128)(4,1)S(1)}, pred[8,17]{0,1:T(8,128)(4,1)}, u32[]{:S(2)}) copy-start(pred[8,17]{0,1:T(8,128)(4,1)} %constant.15) | copy-start | bytes 412
  119.2 17.1 %copy-start.3 = (f32[128]{0:T(128)S(1)}, f32[128]{0:T(128)}, u32[]{:S(2)}) copy-start(f32[128]{0:T(128)} %param.6) | copy-start | bytes 1540
Sparse Core Ops, SparseCore 0:
  10.2 48.6 all-gather.1
  106.8 133.5 all-reduce.2
where the time goes:
time: 255 us
  waiting for transfers between devices  125 us (49%)
  local copies, waits for them, and re-layouts  73.5 us (29%)
  matrix products  37.5 us (15%)
  between operations  14.2 us (6%)
  starting transfers between devices  3.13 us (1%)
    psum x1, waiting for transfers between devices, on_device(): weight_grad = lax.psum(partial_grads, 'space')  101 us
    unnamed x43, local copies, waits for them, and re-layouts  64.7 us
    all_gather x1, waiting for transfers between devices, on_device(): whole = lax.all_gather(volume, 'filt', axis=0, tiled=True)  24.5 us
    dot_general x1, matrix products, tap_grads(): lax.dot_general(slopes, flat, (((1,), (1,)), ((), ())), preferred_element...  20.7 us
    conv_general_dilated x1, matrix products, convolve(): lax.conv_general_dilated(slab[None], kernel, (1, 1, 1), [(0, 0), (1, 1),...  16.9 us
  transfers between devices with their start and end apart: 4, of which 2 were waited for; matrix products, arithmetic and copies ran while one was open for 31% of the time, Pallas kernels for 0%

commit v1 on v0

--- a/solution.py
+++ b/solution.py
@@ -2,6 +2,19 @@
 import jax.numpy as jnp
 from jax import lax
 from jax.sharding import PartitionSpec as P
+
+
+def ring_gather(value, axis, dim):
+    ways = lax.axis_size(axis)
+    up = [(d, (d + 1) % ways) for d in range(ways)]
+    down = [(d, (d - 1) % ways) for d in range(ways)]
+    earlier, later = ([value], [value])
+    for _ in range(ways // 2):
+        earlier.append(lax.ppermute(earlier[-1], axis, up))
+    for _ in range((ways - 1) // 2):
+        later.append(lax.ppermute(later[-1], axis, down))
+    line = jnp.concatenate([*earlier[::-1], *later[1:]], axis=dim)
+    return jnp.roll(line, (lax.axis_index(axis) - ways // 2) * value.shape[dim], axis=dim)
 
 
 def padded(block, sides, width):
@@ -64,7 +77,7 @@
     in_all = weight.shape[2]
     kernel = weight.reshape(out_dev, 3, 3, 3, in_all).transpose(0, 4, 1, 2, 3)
     slopes = shifted_slopes(upstream)
-    whole = lax.all_gather(volume, "filt", axis=0, tiled=True)
+    whole = ring_gather(volume, "filt", 0)
     rimmed = padded(whole, (("space", 1),), 1)
     pre = convolve(rimmed, kernel)
     partial_grads = tap_grads(rimmed, slopes, out_dev)

time: 255 us -> 245 us (0.961)
  local copies, waits for them, and re-layouts: 73.5 us -> 63.7 us
  waiting for transfers between devices: 125 us -> 116 us
  starting transfers between devices: 3.13 us -> 7.92 us
  other arithmetic: 0.96 us -> 4.76 us
    all_gather x1 -> x0, waiting for transfers between devices: 24.5 us -> none  [on_device(): whole = lax.all_gather(volume, 'filt', axis=0, tiled=True)]
    ppermute x0 -> x3, waiting for transfers between devices: none -> 16.4 us  [the longest x2 16.4 us: ring_gather(): earlier.append(lax.ppermute(earlier[-1], axis, up))]
    unnamed x43 -> x56, local copies, waits for them, and re-layouts: 64.7 us -> 56.4 us
    ppermute x0 -> x3, starting transfers between devices: none -> 5.05 us  [the longest x2 3.03 us: ring_gather(): earlier.append(lax.ppermute(earlier[-1], axis, up))]
    broadcast_in_dim x0 -> x1, other arithmetic: none -> 3.8 us  [convolve(): slab[None]]
  transfers between devices with their start and end apart: 4 -> 6, of which waited for: 2 -> 3; matrix products, arithmetic and copies ran while one was open for 31% -> 24% of each run, Pallas kernels for 0% -> 0%
where the time goes in v1:
time: 245 us
  waiting for transfers between devices  116 us (47%)
  local copies, waits for them, and re-layouts  63.7 us (26%)
  matrix products  37.5 us (15%)
  between operations  14.4 us (6%)
  starting transfers between devices  7.92 us (3%)
  other arithmetic  4.76 us (2%)
    psum x1, waiting for transfers between devices, on_device(): weight_grad = lax.psum(partial_grads, 'space')  99.8 us
    unnamed x56, local copies, waits for them, and re-layouts  56.4 us
    dot_general x1, matrix products, tap_grads(): lax.dot_general(slopes, flat, (((1,), (1,)), ((), ())), preferred_element...  20.6 us
    conv_general_dilated x1, matrix products, convolve(): lax.conv_general_dilated(slab[None], kernel, (1, 1, 1), [(0, 0), (1, 1),...  16.9 us
    ppermute x2, waiting for transfers between devices, ring_gather(): earlier.append(lax.ppermute(earlier[-1], axis, up))  16.4 us
  transfers between devices with their start and end apart: 6, of which 3 were waited for; matrix products, arithmetic and copies ran while one was open for 24% of the time, Pallas kernels for 0%

profile of v1, /device:TPU:0, one launch (start us, length us, event | category | flops | bytes accessed | tf_op | source)
XLA Modules:
  0.0 244.5 jit_solution(12869868688648636536)
XLA Ops:
  7.2 2.1 copy.11
  9.3 3.0 %collective-permute-start = (bf16[128,2,8,128]{3,0,2,1:T(8,128)(2,1)}, bf16[128,2,8,128]{3,0,2,1:T(8,128)(2,1)}, u32[]{:S(2)}, u32[]{:S(2)}) collective-permute-start(bf16[128,2,8,128]{3,0,2,1:T(8,128)(2,1)} %copy.11), channel_id=1, source_target_pairs={{0,4},{4,8},{8,12},{12,0},{1,5},{5,9},{9,13},{13,1},{2,6},{6,10},{... | collective-permute-start | bytes 1572872 | tf_op jit(solution)/shard_map/ppermute | solution.py:13
  12.4 2.0 collective-permute-start.2
  14.4 1.2 copy.19
  22.0 5.5 %collective-permute-done = bf16[128,2,8,128]{3,0,2,1:T(8,128)(2,1)} collective-permute-done((bf16[128,2,8,128]{3,0,2,1:T(8,128)(2,1)}, bf16[128,2,8,128]{3,0,2,1:T(8,128)(2,1)}, u32[]{:S(2)}, u32[]{:S(2)}) %collective-permute-start) | collective-permute-done | bytes 524320 | tf_op jit(solution)/shard_map/ppermute | solution.py:13
  29.0 9.3 %copy-done.6 = bf16[128,27,4,8,128]{4,0,3,2,1:T(8,128)(2,1)} copy-done((bf16[128,27,4,8,128]{4,0,3,2,1:T(8,128)(2,1)}, bf16[128,27,4,8,128]{4,0,3,2,1:T(8,128)(2,1)S(1)}, u32[]{:S(2)}) %copy-start.6) | copy-done | bytes 28311576
  38.3 10.8 %collective-permute-done.1 = bf16[128,2,8,128]{3,0,2,1:T(8,128)(2,1)} collective-permute-done((bf16[128,2,8,128]{3,0,2,1:T(8,128)(2,1)}, bf16[128,2,8,128]{3,0,2,1:T(8,128)(2,1)}, u32[]{:S(2)}, u32[]{:S(2)}) %collective-permute-start.1) | collective-permute-done | bytes 524320 | tf_op jit(solution)/shard_map/ppermute | solution.py:13
  50.2 1.1 constant_dynamic-update-slice_fusion.6
  51.4 1.2 constant_dynamic-update-slice_fusion.5
  53.7 1.1 constant_dynamic-update-slice_fusion.3
  54.9 1.1 constant_dynamic-update-slice_fusion.2
  56.0 1.2 constant_dynamic-update-slice_fusion.1
  57.2 1.1 constant_dynamic-update-slice_fusion
  58.5 1.4 collective-permute-start.3
  59.9 1.5 collective-permute-start.4
  61.4 1.3 fusion.60
  62.7 1.3 fusion.62
  64.0 1.2 fusion.64
  65.1 1.3 fusion.66
  66.5 1.4 fusion.68
  67.8 1.1 fusion.70
  68.9 1.3 fusion.72
  70.4 1.4 copy-done.3
  73.1 20.6 %fusion.10 = f32[128,27,512]{2,0,1:T(8,128)} fusion(bf16[128,27,4,8,128]{4,0,3,2,1:T(8,128)(2,1)} %fusion.72, bf16[512,1,8,128]{3,0,2,1:T(8,128)(2,1)S(1)} %collective-permute-done.4, bf16[512,2,8,128]{3,0,2,1:T(8,128)(2,1)S(1)} %constant_dynamic-slice_fusion.2, bf16[512,1,8,128]{3,0,2,1:T(8,128)(2,1)S(1)} %collective-permute-done.3), kind=kOutput, calls=%fused_computation.39 | convolution fusion | flops 14499708928 | bytes 39583744 | tf_op jit(solution)/shard_map/dot_general | solution.py:69
  93.7 3.8 %fusion.14 = bf16[512,4,8,1,128]{4,0,2,1,3:T(8,128)(2,1)} fusion(bf16[512,1,8,128]{3,0,2,1:T(8,128)(2,1)} %copy-done.5, bf16[512,2,8,128]{3,0,2,1:T(8,128)(2,1)} %copy-done.3, bf16[512,1,8,128]{3,0,2,1:T(8,128)(2,1)} %copy-done.4), kind=kLoop, calls=%fused_computation.41 | loop fusion | flops 4194304 | bytes 8388608 | tf_op jit(solution)/shard_map/broadcast_in_dim | solution.py:35
  97.5 8.1 %copy.24 = bf16[512,4,8,1,128]{0,2,4,1,3:T(8,128)(2,1)} copy(bf16[512,4,8,1,128]{4,0,2,1,3:T(8,128)(2,1)} %fusion.14) | data formatting | bytes 8388608
  105.6 2.5 %pad.5.clone = bf16[512,4,8,1,136]{0,2,4,1,3:T(8,128)(2,1)S(1)} pad(bf16[512,4,8,1,128]{0,2,4,1,3:T(8,128)(2,1)} %copy.24, bf16[]{:T(256)} %constant.38.clone.1), padding=0_0x0_0x0_0x0_0x1_7 | pad | bytes 8650754 | tf_op jit(solution)/shard_map/broadcast_in_dim | solution.py:35
  108.2 1.7 copy.17
  110.1 16.9 %fusion.15 = f32[2,8,8,17,128]{4,2,3,1,0:T(8,128)S(1)} fusion(bf16[128,3,3,3,512]{4,0,3,2,1:T(8,128)(2,1)S(1)} %bitcast.143, bf16[512,4,8,1,7,2]{0,4,5,2,1,3:T(8,128)(2,1)S(1)} %slice.118, bf16[512,4,8,1,8,17]{0,4,5,2,1,3:T(8,128)(2,1)S(1)} %copy.17, pred[8,17]{0,1:T(8,128)(4,1)S(1)} %copy-done.8), kind=kOutput, calls=%fused_computation.42 | convolution fusion | flops 7074234368 | bytes 9568392 | tf_op jit(solution)/shard_map/conv_general_dilated | solution.py:34
  128.2 2.4 copy.20
  130.5 99.8 %all-reduce.3.cloned.1.call-done = f32[128,27,512]{2,0,1:T(8,128)} async-done(((f32[128,27,512]{2,0,1:T(8,128)}), f32[128,27,512]{2,0,1:T(8,128)}) %all-reduce.3.cloned.1.call-update) | async-done | bytes 7077904 | tf_op jit(solution)/shard_map/psum | solution.py:84
  230.4 7.3 %copy.61 = f32[128,27,512]{2,0,1:T(8,128)} copy(f32[128,27,512]{2,0,1:T(8,128)} %all-reduce.3.cloned.1.call-done) | data formatting | bytes 14155776
  (49 shorter events, 12.9 us)
Async XLA Ops:
  7.2 102.9 %copy-start = (bf16[128,27,512]{2,0,1:T(8,128)(2,1)S(1)}, bf16[128,27,512]{2,0,1:T(8,128)(2,1)}, u32[]{:S(2)}) copy-start(bf16[128,27,512]{2,0,1:T(8,128)(2,1)} %param.5) | copy-start | bytes 10616836
  7.2 223.2 %all-reduce.3.cloned.1.call-start = ((), (), s32[]{:S(2)}) async-start(), calls=%async_computation | async-start | bytes 14155776 | tf_op jit(solution)/shard_map/psum | solution.py:84
  9.3 18.2 %collective-permute-start = (bf16[128,2,8,128]{3,0,2,1:T(8,128)(2,1)}, bf16[128,2,8,128]{3,0,2,1:T(8,128)(2,1)}, u32[]{:S(2)}, u32[]{:S(2)}) collective-permute-start(bf16[128,2,8,128]{3,0,2,1:T(8,128)(2,1)} %copy.11), channel_id=1, source_target_pairs={{0,4},{4,8},{8,12},{12,0},{1,5},{5,9},{9,13},{13,1},{2,6},{6,10},{... | collective-permute-start | bytes 1572872 | tf_op jit(solution)/shard_map/ppermute | solution.py:13
  12.4 40.2 %collective-permute-start.2 = (bf16[128,2,8,128]{3,0,2,1:T(8,128)(2,1)}, bf16[128,2,8,128]{3,0,2,1:T(8,128)(2,1)}, u32[]{:S(2)}, u32[]{:S(2)}) collective-permute-start(bf16[128,2,8,128]{3,0,2,1:T(8,128)(2,1)} %copy.11), channel_id=1, source_target_pairs={{0,12},{4,0},{8,4},{12,8},{1,13},{5,1},{9,5},{13,9},{2,14},{6,2},{... | collective-permute-start | bytes 1572872 | tf_op jit(solution)/shard_map/ppermute | solution.py:15
  15.6 13.1 %copy-start.1 = (bf16[128,2,8,128]{3,0,2,1:T(8,128)(2,1)}, bf16[128,2,8,128]{3,0,2,1:T(8,128)(2,1)S(1)}, u32[]{:S(2)}) copy-start(bf16[128,2,8,128]{3,0,2,1:T(8,128)(2,1)S(1)} %copy.19) | copy-start | bytes 1572868
  27.5 21.6 %collective-permute-start.1 = (bf16[128,2,8,128]{3,0,2,1:T(8,128)(2,1)}, bf16[128,2,8,128]{3,0,2,1:T(8,128)(2,1)}, u32[]{:S(2)}, u32[]{:S(2)}) collective-permute-start(bf16[128,2,8,128]{3,0,2,1:T(8,128)(2,1)} %collective-permute-done), channel_id=1, source_target_pairs={{0,4},{4,8},{8,12},{12,0},{1,5},{5,9},{9,13},{13,1},{2,6},{6,10},{... | collective-permute-start | bytes 1572872 | tf_op jit(solution)/shard_map/ppermute | solution.py:13
  29.0 9.3 %copy-start.6 = (bf16[128,27,4,8,128]{4,0,3,2,1:T(8,128)(2,1)}, bf16[128,27,4,8,128]{4,0,3,2,1:T(8,128)(2,1)S(1)}, u32[]{:S(2)}) copy-start(bf16[128,27,4,8,128]{4,0,3,2,1:T(8,128)(2,1)S(1)} %fusion.58) | copy-start | bytes 84934656
  38.3 23.1 %copy-start.2 = (bf16[128,2,8,128]{3,0,2,1:T(8,128)(2,1)S(1)}, bf16[128,2,8,128]{3,0,2,1:T(8,128)(2,1)}, u32[]{:S(2)}) copy-start(bf16[128,2,8,128]{3,0,2,1:T(8,128)(2,1)} %copy-done.1) | copy-start | bytes 1572868
  58.5 11.8 %collective-permute-start.3 = (bf16[512,1,8,128]{3,0,2,1:T(8,128)(2,1)S(1)}, bf16[512,1,8,128]{3,0,2,1:T(8,128)(2,1)S(1)}, u32[]{:S(2)}, u32[]{:S(2)}) collective-permute-start(bf16[512,1,8,128]{3,0,2,1:T(8,128)(2,1)S(1)} %get-tuple-element.4), channel_id=1, source_target_pairs={{0,1},{1,2},{2,3},{4,5},{5,6},{6,7},{8,9},{9,10},{10,11},{12,13},{... | collective-permute-start | bytes 3145736 | tf_op jit(solution)/shard_map/ppermute | solution.py:25
  59.9 10.5 %collective-permute-start.4 = (bf16[512,1,8,128]{3,0,2,1:T(8,128)(2,1)S(1)}, bf16[512,1,8,128]{3,0,2,1:T(8,128)(2,1)S(1)}, u32[]{:S(2)}, u32[]{:S(2)}) collective-permute-start(bf16[512,1,8,128]{3,0,2,1:T(8,128)(2,1)S(1)} %get-tuple-element.5), channel_id=1, source_target_pairs={{1,0},{2,1},{3,2},{5,4},{6,5},{7,6},{9,8},{10,9},{11,10},{13,12},{... | collective-permute-start | bytes 3145736 | tf_op jit(solution)/shard_map/ppermute | solution.py:28
  70.4 1.5 copy-start.3
  70.4 1.7 copy-start.4
  72.1 1.0 copy-start.5
  108.2 1.9 copy-start.8
  110.1 17.2 %copy-start.7 = (f32[128]{0:T(128)S(1)}, f32[128]{0:T(128)}, u32[]{:S(2)}) copy-start(f32[128]{0:T(128)} %param.6) | copy-start | bytes 1540
Sparse Core Ops, SparseCore 0:
  93.8 136.4 all-reduce.2
